TPU v7x, 256 devices: a whole 4x4x8 slice. The times are simulated.
256 devices in a mesh: row: 16 (over z_lo, x, core), col: 16 (over z_hi, y).
Axes of the slice: x: 4, y: 4, z: 8 (z_hi: 4, z_lo: 2; z = z_hi * 2 + z_lo), core: 2. Of those that a mesh axis runs over, the one named last changes fastest.
Arguments:
- features: bfloat16 [65536, 512], P(('col', 'row')), may hold values from -6 to 6
- weight: bfloat16 [512, 512], replicated, may hold values from -0.25 to 0.25
- entry_values: bfloat16 [16, 16, 32, 128, 128], P('row', 'col'), may hold values from 0.0009994507 to 0.019897461
- block_rows: int32 [16, 16, 32], P('row', 'col'), may hold values from 0 to 31
- block_cols: int32 [16, 16, 32], P('row', 'col'), may hold values from 0 to 31
- entry_counts: int32 [16, 16], P('row', 'col'), may hold values from 8 to 32, as said below
- cotangent: bfloat16 [65536, 512], P(('row', 'col')), may hold values from -1.5 to 1.5
Outputs:
- output: bfloat16 [65536, 512], P(('row', 'col'))
- grad_features: bfloat16 [65536, 512], P(('col', 'row'))
- grad_weight: float32 [512, 512], replicated
Inputs may be any that keep to these rules, and one draw needn't show every extreme that they name: `entry_counts`: each grid cell has at least 8 live slots; at least one cell has all 32 live.
All inputs are finite; a program needn't handle non-finite values.
Results may differ from a plain program's by a relative error of at most 0.022.
Values may be sent and summed in bfloat16 or wider, within the bound.
No kernel may reach another device: no remote copies, remote signals or barrier semaphores. Data moves between devices by JAX's collectives and lax.ppermute only.
A program may use at most 128 MiB of HBM per device.

v0:
```python
import jax
import jax.numpy as jnp
from jax import lax
from jax.sharding import PartitionSpec as P


def block_terms(values, source_ids, target_ids, live_count, source, target_blocks, transpose):
    entry_total = values.shape[0]
    block_side = values.shape[1]
    feature_count = source.shape[1]
    group_size = min(32, entry_total)
    source_tiles = source.reshape(-1, block_side, feature_count)

    def one_group(group_index, running):
        first_entry = group_index * group_size
        tiles = jnp.take(source_tiles, source_ids, axis=0)
        if transpose:
            products = jnp.einsum("kba,kbf->kaf", values, tiles, preferred_element_type=jnp.float32)
        else:
            products = jnp.einsum("kab,kbf->kaf", values, tiles, preferred_element_type=jnp.float32)
        alive_mask = (first_entry + jnp.arange(group_size) < live_count).astype(jnp.float32)
        return running.at[target_ids].add(products * alive_mask[:, None, None])

    zero_sum = jnp.zeros((target_blocks, block_side, feature_count), jnp.float32)
    trip_count = entry_total // group_size
    running = lax.fori_loop(0, trip_count, one_group, zero_sum)
    return running.reshape(target_blocks * block_side, feature_count)


def silu_slope(summed):
    sigmoid_value = jax.nn.sigmoid(summed)
    return sigmoid_value * (1.0 + summed * (1.0 - sigmoid_value))


def shards(features, weight, entry_values, block_rows, block_cols, entry_counts, cotangent):
    values = entry_values[0, 0]
    row_ids = block_rows[0, 0]
    col_ids = block_cols[0, 0]
    live_count = entry_counts[0, 0]
    local_rows = features.shape[0]
    block_side = values.shape[1]
    row_span = lax.axis_size("col") * local_rows
    col_span = lax.axis_size("row") * local_rows
    projected = jnp.dot(features, weight, preferred_element_type=jnp.float32).astype(jnp.bfloat16)
    panel = lax.all_gather(projected, "row", axis=0, tiled=True)
    forward_terms = block_terms(
        values, col_ids, row_ids, live_count, panel, row_span // block_side, False
    )
    summed = lax.psum(forward_terms.astype(jnp.bfloat16), "col").astype(jnp.float32)
    position = lax.axis_index("col") * local_rows
    own_sum = lax.dynamic_slice_in_dim(summed, position, local_rows, 0)
    output = jax.nn.silu(own_sum).astype(jnp.bfloat16)
    incoming = lax.all_gather(cotangent, "col", axis=0, tiled=True)
    upstream = (incoming.astype(jnp.float32) * silu_slope(summed)).astype(jnp.bfloat16)
    backward_terms = block_terms(
        values, row_ids, col_ids, live_count, upstream, col_span // block_side, True
    )
    grad_projected = lax.psum_scatter(
        backward_terms.astype(jnp.bfloat16), "row", scatter_dimension=0, tiled=True
    )
    weight_term = lax.dot_general(
        features, grad_projected, (((0,), (0,)), ((), ())), preferred_element_type=jnp.float32
    )
    grad_weight = lax.psum(weight_term, ("row", "col"))
    grad_features = lax.dot_general(
        grad_projected, weight, (((1,), (1,)), ((), ())), preferred_element_type=jnp.float32
    ).astype(jnp.bfloat16)
    return (output, grad_features, grad_weight)


def solution(mesh):
    placed = (
        P(("col", "row"), None),
        P(),
        P("row", "col", None, None, None),
        P("row", "col", None),
        P("row", "col", None),
        P("row", "col"),
        P(("row", "col"), None),
    )
    return jax.shard_map(
        shards,
        mesh=mesh,
        in_specs=placed,
        out_specs=(P(("row", "col"), None), P(("col", "row"), None), P()),
        check_vma=False,
    )
```

profile of v0, /device:TPU:2, one launch (start us, length us, event | category | flops | bytes accessed | tf_op | source)
XLA Modules:
  0.0 751.3 jit_solution(11538004060448155654)
XLA Ops:
  7.2 0.0 copy-start
  7.2 0.0 all-gather.3.cloned.1.call-start
  7.2 2.2 convolution_convert_fusion.1
  9.4 0.0 all-gather.3.cloned.1.call-update
  9.5 0.0 all-gather.5.cloned.1.call-start
  9.5 0.7 all-gather.5.cloned.1.call-update
  10.2 0.0 all-reduce.3.cloned.1.call-start
  10.9 0.7 compare_select_fusion.1
  11.6 0.7 fusion.14
  12.2 0.7 compare_and_fusion.1
  12.9 39.9 %all-gather.3.cloned.1.call-done = bf16[4096,512]{1,0:T(8,128)(2,1)} async-done(((bf16[256,512]{1,0:T(8,128)(2,1)}), bf16[4096,512]{1,0:T(8,128)(2,1)}) %all-gather.3.cloned.1.call-update) | async-done | bytes 4194320 | tf_op jit(solution)/shard_map/all_gather | solution.py:45
  52.8 5.0 gather_fusion
  57.8 0.0 copy-done
  57.8 7.1 multiply_bitcast_fusion.1
  64.9 9.1 %copy.14 = f32[32,128,512]{2,1,0:T(8,128)} copy(f32[32,128,512]{1,2,0:T(8,128)} %multiply_bitcast_fusion.1) | data formatting | bytes 16777216 | tf_op jit(solution)/shard_map/while/body/eval_jaxpr/mul | solution.py:22
  74.0 4.3 broadcast.57.clone
  78.2 18.3 %scatter_fusion = f32[32,128,512]{2,1,0:T(8,128)} fusion(f32[32,128,512]{2,1,0:T(8,128)} %broadcast.57.clone, s32[32]{0:T(128)S(1)} %fusion.14, f32[32,128,512]{2,1,0:T(8,128)} %copy.14), kind=kCustom, calls=%fused_computation.2 | custom fusion | flops 2097152 | bytes 25165952 | tf_op jit(solution)/shard_map/while/body/eval_jaxpr/scatter-add | solution.py:22
  96.5 0.0 copy-start.5
  96.5 0.0 copy-start.4
  96.5 6.0 convert_element_type.42
  102.5 0.0 all-reduce.3.cloned.1.call-update
  102.5 0.0 reduce-scatter.2.cloned.1.call-start
  102.6 0.0 copy-done.5
  102.6 0.0 copy-done.4
  102.6 28.0 %all-gather.5.cloned.1.call-done = bf16[4096,512]{1,0:T(8,128)(2,1)} async-done(((bf16[256,512]{1,0:T(8,128)(2,1)}), bf16[4096,512]{1,0:T(8,128)(2,1)}) %all-gather.5.cloned.1.call-update) | async-done | bytes 4194320 | tf_op jit(solution)/shard_map/all_gather | solution.py:53
  130.6 224.6 %all-reduce.3.cloned.1.call-done = bf16[4096,512]{1,0:T(8,128)(2,1)} async-done(((bf16[4096,512]{1,0:T(8,128)(2,1)}), bf16[4096,512]{1,0:T(8,128)(2,1)}) %all-reduce.3.cloned.1.call-update) | async-done | bytes 4194320 | tf_op jit(solution)/shard_map/psum | solution.py:49
  355.2 7.0 multiply_convert_fusion
  362.2 5.0 gather_fusion.1
  367.1 7.1 multiply_bitcast_fusion
  374.3 9.0 %copy.16 = f32[32,128,512]{2,1,0:T(8,128)} copy(f32[32,128,512]{1,2,0:T(8,128)} %multiply_bitcast_fusion) | data formatting | bytes 16777216 | tf_op jit(solution)/shard_map/while/body/eval_jaxpr/mul | solution.py:22
  383.3 4.3 broadcast.57
  387.6 18.3 %scatter_fusion.1 = f32[32,128,512]{2,1,0:T(8,128)} fusion(f32[32,128,512]{2,1,0:T(8,128)} %broadcast.57, s32[32]{0:T(128)S(1)} %fusion.15, f32[32,128,512]{2,1,0:T(8,128)} %copy.16), kind=kCustom, calls=%fused_computation.3 | custom fusion | flops 2097152 | bytes 25165952 | tf_op jit(solution)/shard_map/while/body/eval_jaxpr/scatter-add | solution.py:22
  405.9 6.0 convert_element_type.48
  411.9 0.0 reduce-scatter.2.cloned.1.call-update
  411.9 0.0 copy-start.1
  411.9 0.0 all-reduce.5.cloned.1.call-start
  412.0 63.4 %reduce-scatter.2.cloned.1.call-done = bf16[256,512]{1,0:T(8,128)(2,1)} async-done(((bf16[4096,512]{1,0:T(8,128)(2,1)}), bf16[256,512]{1,0:T(8,128)(2,1)}) %reduce-scatter.2.cloned.1.call-update) | async-done | bytes 262160 | tf_op jit(solution)/shard_map/reduce_scatter | solution.py:58
  475.4 0.0 copy-done.2
  475.4 0.0 copy-start.3
  475.4 2.3 convolution_bitcast_fusion
  477.7 0.0 all-reduce.5.cloned.1.call-update
  477.8 3.4 convert_element_type.44
  481.1 0.9 multiply_convert_fusion.1
  482.0 0.0 copy-done.1
  482.0 0.0 copy-done.3
  482.0 1.0 convolution_convert_fusion
  483.0 259.2 %all-reduce.5.cloned.1.call-done = f32[512,512]{0,1:T(8,128)} async-done(((f32[512,512]{0,1:T(8,128)}), f32[512,512]{0,1:T(8,128)}) %all-reduce.5.cloned.1.call-update) | async-done | bytes 1048592 | tf_op jit(solution)/shard_map/psum | solution.py:64
  742.2 2.5 copy.17
  (6 shorter events, 0.0 us)
Async XLA Ops:
  7.2 50.6 %copy-start = (bf16[1,1,32,128,128]{4,3,2,1,0:T(8,128)(2,1)S(1)}, bf16[1,1,32,128,128]{4,3,2,1,0:T(8,128)(2,1)}, u32[]{:S(2)}) copy-start(bf16[1,1,32,128,128]{4,3,2,1,0:T(8,128)(2,1)} %param.11) | copy-start | bytes 3145732
  7.2 45.6 %all-gather.3.cloned.1.call-start = ((), (), s32[]{:S(2)}) async-start(), calls=%async_computation.1 | async-start | bytes 4456448 | tf_op jit(solution)/shard_map/all_gather | solution.py:45
  9.5 121.2 %all-gather.5.cloned.1.call-start = ((), (), s32[]{:S(2)}) async-start(), calls=%async_computation.3 | async-start | bytes 4456448 | tf_op jit(solution)/shard_map/all_gather | solution.py:53
  10.2 345.0 %all-reduce.3.cloned.1.call-start = ((), (), s32[]{:S(2)}) async-start(), calls=%async_computation.2 | async-start | bytes 8388608 | tf_op jit(solution)/shard_map/psum | solution.py:49
  96.5 6.1 copy-start.5
  96.5 6.1 copy-start.4
  102.5 372.9 %reduce-scatter.2.cloned.1.call-start = ((), (), s32[]{:S(2)}) async-start(), calls=%async_computation.4 | async-start | bytes 4456448 | tf_op jit(solution)/shard_map/reduce_scatter | solution.py:58
  405.9 69.5 %copy-start.2 = (bf16[256,512]{1,0:T(8,128)(2,1)S(1)}, bf16[256,512]{1,0:T(8,128)(2,1)}, u32[]{:S(2)}) copy-start(bf16[256,512]{1,0:T(8,128)(2,1)} %param.9) | copy-start | bytes 786436
  411.9 70.1 %copy-start.1 = (bf16[512,512]{1,0:T(8,128)(2,1)S(1)}, bf16[512,512]{1,0:T(8,128)(2,1)}, u32[]{:S(2)}) copy-start(bf16[512,512]{1,0:T(8,128)(2,1)} %param.10) | copy-start | bytes 1572868
  411.9 330.3 %all-reduce.5.cloned.1.call-start = ((), (), s32[]{:S(2)}) async-start(), calls=%async_computation.5 | async-start | bytes 2097152 | tf_op jit(solution)/shard_map/psum | solution.py:64
  475.4 6.6 copy-start.3
Sparse Core Ops, SparseCore 0:
  10.4 42.3 all-gather.2
  55.2 75.3 all-gather.4
  133.3 221.8 all-reduce.2
  412.1 63.2 reduce-scatter.1
  481.3 260.9 all-reduce.4
where the time goes:
time: 752 us; the launch traced here: 751 us
  waiting for transfers between devices  616 us (82%)
  other arithmetic  61.8 us (8%)
  local copies, waits for them, and re-layouts  39.2 us (5%)
  matrix products  19.8 us (3%)
  between operations  14.5 us (2%)
    psum x1, waiting for transfers between devices, shards(): grad_weight = lax.psum(weight_term, ('row', 'col'))  259 us
    psum x1, waiting for transfers between devices, shards(): lax.psum(forward_terms.astype(jnp.bfloat16), 'col').astype(jnp.float32)  225 us
    reduce_scatter x1, waiting for transfers between devices, shards(): lax.psum_scatter(backward_terms.astype(jnp.bfloat16), 'row', scatter_dime...  63.4 us
    all_gather x1, waiting for transfers between devices, shards(): panel = lax.all_gather(projected, 'row', axis=0, tiled=True)  39.9 us
    scatter-add x2, other arithmetic, one_group(): return running.at[target_ids].add(products * alive_mask[:, None, None])  36.6 us
    all_gather x1, waiting for transfers between devices, shards(): incoming = lax.all_gather(cotangent, 'col', axis=0, tiled=True)  28 us
    mul x2, local copies, waits for them, and re-layouts, one_group(): return running.at[target_ids].add(products * alive_mask[:, None, None])  18.1 us
  transfers between devices with their start and end apart: 5, of which 5 were waited for; matrix products, arithmetic and copies ran while one was open for 8% of the time, Pallas kernels for 0%

commit v1 on v0

--- a/solution.py
+++ b/solution.py
@@ -42,7 +42,16 @@
     row_span = lax.axis_size("col") * local_rows
     col_span = lax.axis_size("row") * local_rows
     projected = jnp.dot(features, weight, preferred_element_type=jnp.float32).astype(jnp.bfloat16)
-    panel = lax.all_gather(projected, "row", axis=0, tiled=True)
+    do_joints_on_mesh = lambda view: jnp.concatenate(
+        lax.all_to_all(
+            jnp.stack([view] * lax.axis_size("row"), axis=0),
+            concat_axis=0,
+            axis_name="row",
+            split_axis=0,
+        ),
+        axis=0,
+    )
+    panel = do_joints_on_mesh(projected)
     forward_terms = block_terms(
         values, col_ids, row_ids, live_count, panel, row_span // block_side, False
     )

time: 752 us -> 778 us (1.035)
  waiting for transfers between devices: 616 us -> 635 us
    all_to_all x0 -> x1, waiting for transfers between devices: none -> 83.8 us  [shards(): lax.all_to_all(jnp.stack([view] * lax.axis_size('row'), axis=0), concat_a...]
    all_gather x1 -> x0, waiting for transfers between devices: 39.9 us -> none  [shards(): panel = lax.all_gather(projected, 'row', axis=0, tiled=True)]
    all_gather x1, waiting for transfers between devices: 28 us -> 0.02 us  [shards(): incoming = lax.all_gather(cotangent, 'col', axis=0, tiled=True)]
  transfers between devices with their start and end apart: 5 -> 5, of which waited for: 5 -> 4; matrix products, arithmetic and copies ran while one was open for 8% -> 7% of each run, Pallas kernels for 0% -> 0%
where the time goes in v1:
time: 778 us; the launch traced here: 777 us
  waiting for transfers between devices  635 us (82%)
  other arithmetic  59.9 us (8%)
  local copies, waits for them, and re-layouts  41.5 us (5%)
  matrix products  19.2 us (2%)
  between operations  14.6 us (2%)
    psum x1, waiting for transfers between devices, shards(): grad_weight = lax.psum(weight_term, ('row', 'col'))  259 us
    psum x1, waiting for transfers between devices, shards(): lax.psum(forward_terms.astype(jnp.bfloat16), 'col').astype(jnp.float32)  228 us
    all_to_all x1, waiting for transfers between devices, shards(): lax.all_to_all(jnp.stack([view] * lax.axis_size('row'), axis=0), concat_a...  83.8 us
    reduce_scatter x1, waiting for transfers between devices, shards(): lax.psum_scatter(backward_terms.astype(jnp.bfloat16), 'row', scatter_dime...  63.6 us
    scatter-add x2, other arithmetic, one_group(): return running.at[target_ids].add(products * alive_mask[:, None, None])  36.7 us
    mul x2, local copies, waits for them, and re-layouts, one_group(): return running.at[target_ids].add(products * alive_mask[:, None, None])  18.1 us
  transfers between devices with their start and end apart: 5, of which 4 were waited for; matrix products, arithmetic and copies ran while one was open for 7% of the time, Pallas kernels for 0%

profile of v1, /device:TPU:2, one launch (start us, length us, event | category | flops | bytes accessed | tf_op | source)
XLA Modules:
  0.0 777.4 jit_solution(4520642364028519135)
XLA Ops:
  7.2 0.0 copy-start
  7.2 0.0 copy-start.4
  7.2 0.0 copy-start.5
  7.2 1.5 convolution_convert_fusion.1
  8.7 2.4 stack.2
  11.1 6.5 all-to-all-start
  17.6 0.0 all-gather.2.cloned.1.call-start
  17.7 0.7 all-gather.2.cloned.1.call-update
  18.3 0.0 all-reduce.3.cloned.1.call-start
  19.0 0.0 copy-done.4
  19.1 0.0 copy-done.5
  19.1 83.8 %all-to-all-done = bf16[16,256,512]{2,1,0:T(8,128)(2,1)} async-done(((bf16[16,256,512]{2,1,0:T(8,128)(2,1)}), bf16[16,256,512]{2,1,0:T(8,128)(2,1)}, u32[]{:S(2)}, u32[]{:S(2)}) %all-to-all-start) | async-done | bytes 4194336 | tf_op jit(solution)/shard_map/all_to_all | solution.py:46
  102.9 5.0 gather_fusion
  107.8 0.0 copy-done
  107.8 7.2 multiply_bitcast_fusion.1
  115.1 9.0 %copy.14 = f32[32,128,512]{2,1,0:T(8,128)} copy(f32[32,128,512]{1,2,0:T(8,128)} %multiply_bitcast_fusion.1) | data formatting | bytes 16777216 | tf_op jit(solution)/shard_map/while/body/eval_jaxpr/mul | solution.py:22
  124.1 4.3 broadcast.59.clone
  128.4 18.4 %scatter_fusion = f32[32,128,512]{2,1,0:T(8,128)} fusion(f32[32,128,512]{2,1,0:T(8,128)} %broadcast.59.clone, s32[32]{0:T(128)S(1)} %fusion.14, f32[32,128,512]{2,1,0:T(8,128)} %copy.14), kind=kCustom, calls=%fused_computation.2 | custom fusion | flops 2097152 | bytes 25165952 | tf_op jit(solution)/shard_map/while/body/eval_jaxpr/scatter-add | solution.py:22
  146.8 6.0 convert_element_type.42
  152.7 0.0 all-reduce.3.cloned.1.call-update
  152.7 0.2 reduce-scatter.2.cloned.1.call-start
  153.0 0.0 all-gather.2.cloned.1.call-done
  153.1 227.9 %all-reduce.3.cloned.1.call-done = bf16[4096,512]{1,0:T(8,128)(2,1)} async-done(((bf16[4096,512]{1,0:T(8,128)(2,1)}), bf16[4096,512]{1,0:T(8,128)(2,1)}) %all-reduce.3.cloned.1.call-update) | async-done | bytes 4194320 | tf_op jit(solution)/shard_map/psum | solution.py:58
  381.0 7.0 multiply_convert_fusion
  388.0 5.0 gather_fusion.1
  392.9 7.1 multiply_bitcast_fusion
  400.1 9.0 %copy.16 = f32[32,128,512]{2,1,0:T(8,128)} copy(f32[32,128,512]{1,2,0:T(8,128)} %multiply_bitcast_fusion) | data formatting | bytes 16777216 | tf_op jit(solution)/shard_map/while/body/eval_jaxpr/mul | solution.py:22
  409.1 4.3 broadcast.59
  413.4 18.3 %scatter_fusion.1 = f32[32,128,512]{2,1,0:T(8,128)} fusion(f32[32,128,512]{2,1,0:T(8,128)} %broadcast.59, s32[32]{0:T(128)S(1)} %fusion.15, f32[32,128,512]{2,1,0:T(8,128)} %copy.16), kind=kCustom, calls=%fused_computation.3 | custom fusion | flops 2097152 | bytes 25165952 | tf_op jit(solution)/shard_map/while/body/eval_jaxpr/scatter-add | solution.py:22
  431.7 0.0 copy-start.2
  431.7 6.0 convert_element_type.48
  437.7 0.0 reduce-scatter.2.cloned.1.call-update
  437.7 0.0 copy-start.1
  437.7 0.0 all-reduce.5.cloned.1.call-start
  437.8 63.6 %reduce-scatter.2.cloned.1.call-done = bf16[256,512]{1,0:T(8,128)(2,1)} async-done(((bf16[4096,512]{1,0:T(8,128)(2,1)}), bf16[256,512]{1,0:T(8,128)(2,1)}) %reduce-scatter.2.cloned.1.call-update) | async-done | bytes 262160 | tf_op jit(solution)/shard_map/reduce_scatter | solution.py:67
  501.4 0.0 copy-done.2
  501.4 0.0 copy-start.3
  501.4 2.3 convolution_bitcast_fusion
  503.7 0.0 all-reduce.5.cloned.1.call-update
  503.8 3.4 convert_element_type.44
  507.2 0.9 multiply_convert_fusion.1
  508.0 0.0 copy-done.1
  508.0 0.0 copy-done.3
  508.0 1.0 convolution_convert_fusion
  509.1 259.2 %all-reduce.5.cloned.1.call-done = f32[512,512]{0,1:T(8,128)} async-done(((f32[512,512]{0,1:T(8,128)}), f32[512,512]{0,1:T(8,128)}) %all-reduce.5.cloned.1.call-update) | async-done | bytes 1048592 | tf_op jit(solution)/shard_map/psum | solution.py:73
  768.3 2.5 copy.17
  (8 shorter events, 0.0 us)
Async XLA Ops:
  7.2 100.7 %copy-start = (bf16[1,1,32,128,128]{4,3,2,1,0:T(8,128)(2,1)S(1)}, bf16[1,1,32,128,128]{4,3,2,1,0:T(8,128)(2,1)}, u32[]{:S(2)}) copy-start(bf16[1,1,32,128,128]{4,3,2,1,0:T(8,128)(2,1)} %param.11) | copy-start | bytes 3145732
  7.2 11.9 %copy-start.4 = (s32[1,1,32]{2,1,0:T(1,128)S(1)}, s32[1,1,32]{2,1,0:T(1,128)}, u32[]{:S(2)}) copy-start(s32[1,1,32]{2,1,0:T(1,128)} %param.13) | copy-start | bytes 388
  7.2 11.9 %copy-start.5 = (s32[1,1,32]{2,1,0:T(1,128)S(1)}, s32[1,1,32]{2,1,0:T(1,128)}, u32[]{:S(2)}) copy-start(s32[1,1,32]{2,1,0:T(1,128)} %param.12) | copy-start | bytes 388
  11.1 91.8 %all-to-all-start = ((bf16[16,256,512]{2,1,0:T(8,128)(2,1)}), bf16[16,256,512]{2,1,0:T(8,128)(2,1)}, u32[]{:S(2)}, u32[]{:S(2)}) async-start(bf16[16,256,512]{2,1,0:T(8,128)(2,1)} %stack.2), calls=%async_computation | async-start | bytes 8388608 | tf_op jit(solution)/shard_map/all_to_all | solution.py:46
  17.6 135.4 %all-gather.2.cloned.1.call-start = ((), (), s32[]{:S(2)}) async-start(), calls=%async_computation.3 | async-start | bytes 4456448 | tf_op jit(solution)/shard_map/all_gather | solution.py:62
  18.3 362.7 %all-reduce.3.cloned.1.call-start = ((), (), s32[]{:S(2)}) async-start(), calls=%async_computation.2 | async-start | bytes 8388608 | tf_op jit(solution)/shard_map/psum | solution.py:58
  152.7 348.7 %reduce-scatter.2.cloned.1.call-start = ((), (), s32[]{:S(2)}) async-start(), calls=%async_computation.4 | async-start | bytes 4456448 | tf_op jit(solution)/shard_map/reduce_scatter | solution.py:67
  431.7 69.7 %copy-start.2 = (bf16[256,512]{1,0:T(8,128)(2,1)S(1)}, bf16[256,512]{1,0:T(8,128)(2,1)}, u32[]{:S(2)}) copy-start(bf16[256,512]{1,0:T(8,128)(2,1)} %param.9) | copy-start | bytes 786436
  437.7 70.3 %copy-start.1 = (bf16[512,512]{1,0:T(8,128)(2,1)S(1)}, bf16[512,512]{1,0:T(8,128)(2,1)}, u32[]{:S(2)}) copy-start(bf16[512,512]{1,0:T(8,128)(2,1)} %param.10) | copy-start | bytes 1572868
  437.7 330.6 %all-reduce.5.cloned.1.call-start = ((), (), s32[]{:S(2)}) async-start(), calls=%async_computation.5 | async-start | bytes 2097152 | tf_op jit(solution)/shard_map/psum | solution.py:73
  501.4 6.6 copy-start.3
Sparse Core Ops, SparseCore 0:
  20.8 94.2 all-gather.1
  152.9 228.0 all-reduce.2
  437.9 63.5 reduce-scatter.1
  507.3 260.9 all-reduce.4
